TPU v7x, 32 devices: a whole 2x2x4 slice. The times are simulated.
32 devices in a mesh: uv: 8 (over y, x, core), chan: 4 (over z).
Axes of the slice: x: 2, y: 2, z: 4, core: 2. Of those that a mesh axis runs over, the one named last changes fastest.
Arguments:
- vis: bfloat16 [98304, 2, 1024], P('uv', None, 'chan'), may hold values from -6 to 6
- row_cell: int32 [98304], P('uv'), may hold values from 0 to 127
- tap_weight: bfloat16 [8, 98304], P(None, 'uv'), may hold values from 0.029907227 to 0.29882812
- tap_offset: int32 [8], replicated, may hold values from -32 to 32
- block_tile: int32 [768], P('uv'), may hold values from 0 to 79, as said below
- tile_owner: int32 [80], replicated, may hold values from 0 to 7, as said below
- galaxy: bfloat16 [152, 128, 2048], P('uv', 'chan'), may hold values from -6 to 6
Outputs:
- delay_cube: bfloat16 [152, 128, 2048], P('uv', 'chan')
- cross_power: float32 [152, 1024], P('uv')
Inputs may be any that keep to these rules, and one draw needn't show every extreme that they name: `tile_owner`: each of the 8 owners holds 1 to 19 tiles, and some owner exactly 19. `block_tile`: of the 96 row blocks of one index of uv, at most 22 lie in tiles of one owner, and exactly 22 lie in the tiles of some owner.
All inputs are finite; a program needn't handle non-finite values.
Results may differ from a plain program's by a relative error of at most 0.0059.
Values may be sent and summed in bfloat16 or wider, within the bound.
No kernel may reach another device: no remote copies, remote signals or barrier semaphores. Data moves between devices by JAX's collectives and lax.ppermute only.
A program may use at most 128 MiB of HBM per device.

v0:
```python
import math
import jax
import jax.numpy as jnp
from jax import lax
from jax.sharding import PartitionSpec as P

CH = 1024
BR = 128
TC = 128
KT = 8
TILES_DEV = 10


def tile_ranks(tile_owner, owners):
    onehot = (tile_owner[:, None] == jnp.arange(owners, dtype=jnp.int32)[None, :]).astype(jnp.int32)
    before = jnp.cumsum(onehot, axis=0) - onehot
    return jnp.sum(before * onehot, axis=1)


def kernel_matrix(cells, weights, tap_offset):
    positions = jnp.arange(TC, dtype=jnp.int32)
    total = jnp.zeros(cells.shape[:-1] + (TC, cells.shape[-1]), jnp.float32)
    for k in range(KT):
        target = cells + tap_offset[k]
        hit = target[..., None, :] == positions[:, None]
        total = total + jnp.where(
            hit, weights[..., k, :].astype(jnp.float32)[..., None, :], jnp.float32(0.0)
        )
    return total.astype(jnp.bfloat16)


def delay_table():
    freq = jnp.arange(CH, dtype=jnp.int32)
    phase = (freq[:, None] * freq[None, :] % CH).astype(jnp.float32) * jnp.float32(
        2.0 * math.pi / CH
    )
    cosine = jnp.cos(phase)
    sine = jnp.sin(phase)
    x = freq.astype(jnp.float32) * jnp.float32(2.0 * math.pi / CH)
    taper = 0.35875 - 0.48829 * jnp.cos(x) + 0.14128 * jnp.cos(2.0 * x) - 0.01168 * jnp.cos(3.0 * x)
    scale = (taper / jnp.float32(math.sqrt(CH)))[:, None]
    upper = jnp.concatenate([cosine * scale, -sine * scale], axis=1)
    lower = jnp.concatenate([sine * scale, cosine * scale], axis=1)
    return jnp.concatenate([upper, lower], axis=0).astype(jnp.bfloat16)


def body(vis, row_cell, tap_weight, tap_offset, block_tile, tile_owner, galaxy):
    n_owners = lax.axis_size("uv")
    nblocks = block_tile.shape[0]
    mean_load = nblocks // n_owners
    capacity = mean_load + (TILES_DEV - 1) * mean_load // TILES_DEV
    slots_dev = 2 * TILES_DEV - 1
    chan_dev = vis.shape[2]
    buffer_size = n_owners * capacity
    rank_of_tile = tile_ranks(tile_owner, n_owners)
    target_owner = tile_owner[block_tile]
    owner_hot = (target_owner[:, None] == jnp.arange(n_owners, dtype=jnp.int32)[None, :]).astype(
        jnp.int32
    )
    earlier = jnp.cumsum(owner_hot, axis=0) - owner_hot
    place = target_owner * capacity + jnp.sum(earlier * owner_hot, axis=1)
    blocks = vis.reshape(nblocks, BR, 2 * chan_dev)
    cells = row_cell.reshape(nblocks, BR)
    weights = jnp.transpose(tap_weight.reshape(KT, nblocks, BR), (1, 0, 2))
    sent_vis = jnp.zeros((buffer_size, BR, 2 * chan_dev), jnp.bfloat16).at[place].set(blocks)
    sent_tile = jnp.full((buffer_size,), -1, jnp.int32).at[place].set(block_tile)
    sent_cells = jnp.zeros((buffer_size, BR), jnp.int32).at[place].set(cells)
    sent_weights = jnp.zeros((buffer_size, KT, BR), jnp.bfloat16).at[place].set(weights)
    got_vis, got_tile, got_cells, got_weights = (
        lax.all_to_all(sent_vis, "uv", split_axis=0, concat_axis=0, tiled=True),
        lax.all_to_all(sent_tile, "uv", split_axis=0, concat_axis=0, tiled=True),
        lax.all_to_all(sent_cells, "uv", split_axis=0, concat_axis=0, tiled=True),
        lax.all_to_all(sent_weights, "uv", split_axis=0, concat_axis=0, tiled=True),
    )
    got_matrix = kernel_matrix(got_cells, got_weights, tap_offset)
    contrib = jnp.einsum("bcr,brf->bcf", got_matrix, got_vis, preferred_element_type=jnp.float32)
    slot = jnp.where(got_tile >= 0, rank_of_tile[jnp.maximum(got_tile, 0)], -1)
    pick = (slot[:, None] == jnp.arange(slots_dev, dtype=jnp.int32)[None, :]).astype(jnp.float32)
    grid = jnp.einsum("bs,bcf->scf", pick, contrib, precision=lax.Precision.HIGHEST)
    gridded = grid.astype(jnp.bfloat16).reshape(slots_dev, TC, 2, chan_dev)
    table = delay_table()
    piece = lax.all_to_all(gridded, "chan", split_axis=1, concat_axis=3, tiled=True)
    count = piece.shape[0]
    cells_part = piece.shape[1]
    flat = piece.reshape(count * cells_part, 2 * CH)
    out = jnp.dot(flat, table, preferred_element_type=jnp.float32)
    delay = out.reshape(count, cells_part, 2 * CH)
    galaxy_f = galaxy.astype(jnp.float32)
    product = delay[..., :CH] * galaxy_f[..., :CH] + delay[..., CH:] * galaxy_f[..., CH:]
    local_power = jnp.sum(product, axis=1)
    power = lax.psum(local_power, "chan") / jnp.float32(math.sqrt(TC))
    return (delay.astype(jnp.bfloat16), power)


def solution(mesh):
    return jax.shard_map(
        body,
        mesh=mesh,
        in_specs=(
            P("uv", None, "chan"),
            P("uv"),
            P(None, "uv"),
            P(),
            P("uv"),
            P(),
            P("uv", "chan", None),
        ),
        out_specs=(P("uv", "chan", None), P("uv", None)),
        check_vma=False,
    )
```

profile of v0, /device:TPU:0, one launch (start us, length us, event | category | flops | bytes accessed | tf_op | source)
XLA Modules:
  0.0 569.6 jit_solution(16998166635543470072)
XLA Ops:
  7.2 0.0 copy-start
  7.2 0.7 compare_select_fusion.1
  7.9 1.6 gather_fusion
  9.4 0.1 fusion.41
  9.5 0.1 reduce_window_sum.22
  9.7 0.2 select_reduce_fusion
  9.9 1.0 scatter_custom_fusion
  10.9 0.7 all_to_all.29
  11.6 5.2 all-to-all-start
  16.8 0.0 copy-done
  16.8 0.8 scatter_custom_fusion.1
  17.6 0.6 all_to_all.31
  18.2 3.1 all-to-all-done
  21.4 3.4 all-to-all-start.1
  24.7 0.8 broadcast_in_dim.144
  25.5 10.6 %scatter_fusion = bf16[176,8,128]{2,1,0:T(8,128)(2,1)} fusion(bf16[176,8,128]{2,1,0:T(8,128)(2,1)} %broadcast_in_dim.144, s32[96]{0:T(128)S(1)} %fusion.47, bf16[96,8,128]{2,1,0:T(8,128)(2,1)} %bitcast.45), kind=kCustom, calls=%fused_computation.4 | custom fusion | bytes 590208 | tf_op jit(solution)/shard_map/scatter | solution.py:68
  36.1 0.0 all-to-all-done.1
  36.1 4.1 all-to-all-start.2
  40.3 20.5 %reshape.204 = bf16[96,128,512]{2,1,0:T(8,128)(2,1)} reshape(bf16[12288,2,256]{2,1,0:T(2,128)(2,1)} %param.7) | data formatting | bytes 25165824 | tf_op jit(solution)/shard_map/reshape | solution.py:62
  60.7 7.9 %broadcast_in_dim.170 = bf16[176,128,512]{2,1,0:T(8,128)(2,1)} broadcast(bf16[]{:T(256)} %constant.24.clone.1), dimensions={} | broadcast | bytes 23068674 | tf_op jit(solution)/shard_map/broadcast_in_dim | solution.py:65
  68.6 33.0 %scatter_fusion.1 = bf16[176,128,512]{2,1,0:T(8,128)(2,1)} fusion(bf16[176,128,512]{2,1,0:T(8,128)(2,1)} %broadcast_in_dim.170, s32[96]{0:T(128)S(1)} %fusion.47, bf16[96,128,512]{2,1,0:T(8,128)(2,1)} %reshape.204), kind=kCustom, calls=%fused_computation.5 | custom fusion | bytes 37749120 | tf_op jit(solution)/shard_map/scatter | solution.py:65
  101.6 0.0 copy-start.2
  101.6 0.0 copy-start.3
  101.6 0.0 all-to-all-done.2
  101.6 6.4 %all-to-all-start.3 = ((bf16[176,128,512]{2,1,0:T(8,128)(2,1)}), bf16[176,128,512]{2,1,0:T(8,128)(2,1)}, u32[]{:S(2)}, u32[]{:S(2)}) async-start(bf16[176,128,512]{2,1,0:T(8,128)(2,1)} %scatter_fusion.1), calls=%async_computation.3 | async-start | bytes 46137344 | tf_op jit(solution)/shard_map/all_to_all | solution.py:70
  108.0 0.0 copy-done.2
  108.1 0.1 fusion.43
  108.1 0.1 reduce_window_sum.23
  108.3 0.0 copy-done.3
  108.3 0.7 fusion.52
  108.9 0.2 select_reduce_fusion.1
  109.1 0.1 reshape.170
  109.2 0.1 ge.11
  109.3 1.6 gather_fusion.1
  110.9 5.1 broadcast_add_fusion.7
  116.2 0.5 slice_convert_fusion.7
  116.6 242.7 %all-to-all-done.3 = bf16[176,128,512]{2,1,0:T(8,128)(2,1)} async-done(((bf16[176,128,512]{2,1,0:T(8,128)(2,1)}), bf16[176,128,512]{2,1,0:T(8,128)(2,1)}, u32[]{:S(2)}, u32[]{:S(2)}) %all-to-all-start.3) | async-done | bytes 23068704 | tf_op jit(solution)/shard_map/all_to_all | solution.py:70
  359.4 29.0 %fusion.9 = f32[176,128,512]{2,1,0:T(8,128)} fusion(bf16[176,128,512]{2,1,0:T(8,128)(2,1)} %all-to-all-done.3, f32[176,128]{1,0:T(8,128)S(1)} %bitcast.47, s32[176,128]{1,0:T(8,128)S(1)} %add.223, f32[176,128]{1,0:T(8,128)S(1)} %bitcast.48, s32[176,128]{1,0:T(8,128)S(1)} %add.219, f32[176,128]{1,0:T(8,128)S(1)} %bitcast.49, s32[176,128]{1,0:T(8,128)S(1)} %add.215, ...), kind=kOutput, calls=%fused_computation.28 | convolution fusion | flops 3021996032 | bytes 70647808 | tf_op jit(solution)/shard_map/bcr,brf->bcf/dot_general | solution.py:76
  388.4 49.7 %fusion.35 = bf16[19,128,512]{2,0,1:T(8,128)(2,1)S(1)} fusion(f32[176,128,512]{2,1,0:T(8,128)} %fusion.9, s32[176]{0:T(256)S(1)} %broadcast_select_fusion), kind=kOutput, calls=%fused_computation.59 | convolution fusion | flops 2631077120 | bytes 48628416 | tf_op jit(solution)/shard_map/bs,bcf->scf/dot_general | solution.py:79
  438.1 3.4 copy.18
  441.5 7.4 %copy.19 = bf16[19,128,2,256]{3,2,0,1:T(2,128)(2,1)} copy(bf16[19,128,2,256]{1,3,2,0:T(8,128)(2,1)} %bitcast.43) | data formatting | bytes 4980736 | tf_op jit(solution)/shard_map/reshape | solution.py:80
  448.9 4.9 all-to-all-start.4
  453.8 0.0 all-reduce.2.cloned.1.call-start
  453.8 4.6 convert_element_type.65
  458.3 0.1 subtract_multiply_fusion
  458.4 19.1 %multiply_convert_fusion.1 = (bf16[1024,1024]{1,0:T(8,128)(2,1)}, bf16[1024,1024]{1,0:T(8,128)(2,1)}, bf16[1024,1024]{1,0:T(8,128)(2,1)}) fusion(f32[1024]{0:T(1024)S(1)} %subtract_multiply_fusion), kind=kLoop, calls=%fused_computation.50 | loop fusion | flops 22020096 | bytes 6295552 | tf_op jit(solution)/shard_map/convert.13
  477.5 30.1 %all-to-all-done.4 = bf16[19,128,2,256]{3,2,0,1:T(2,128)(2,1)S(1)} async-done(((bf16[19,128,2,256]{3,2,0,1:T(2,128)(2,1)}), bf16[19,128,2,256]{3,2,0,1:T(2,128)(2,1)S(1)}, u32[]{:S(2)}, u32[]{:S(2)}) %all-to-all-start.4) | async-done | bytes 2490400 | tf_op jit(solution)/shard_map/all_to_all | solution.py:82
  507.6 0.4 copy.20
  508.1 2.2 copy.21
  510.2 0.0 slice-start
  510.2 3.0 dot_general.13
  513.3 0.0 slice-start.1
  513.3 0.0 copy-start.1
  513.3 11.1 %fusion.53 = (bf16[19,32,2048]{2,1,0:T(8,128)(2,1)}, f32[19,32,2048]{2,1,0:T(8,128)S(1)}) fusion(bf16[19,32,2048]{2,1,0:T(8,128)(2,1)} %dot_general.13, bf16[1024,1024]{1,0:T(8,128)(2,1)} %get-tuple-element.20, bf16[1024,1024]{1,0:T(8,128)(2,1)} %get-tuple-element.19, bf16[1024,1024]{1,0:T(8,128)(2,1)} %get-tuple-element.18), kind=kOutput, calls=%fused_computation.104 | convolution fusion | flops 5135073280 | bytes 16252928 | tf_op jit(solution)/shard_map/dot_general | solution.py:86
  524.3 0.0 slice-done
  524.3 0.0 slice-done.1
  524.3 2.0 fusion.34
  526.3 0.0 all-reduce.2.cloned.1.call-update
  526.4 34.8 %all-reduce.2.cloned.1.call-done = f32[19,1024]{1,0:T(8,128)} async-done(((f32[19,1024]{1,0:T(8,128)}), f32[19,1024]{1,0:T(8,128)}) %all-reduce.2.cloned.1.call-update) | async-done | bytes 77840 | tf_op jit(solution)/shard_map/psum | solution.py:91
  561.2 1.5 broadcast_multiply_fusion
  562.7 0.0 copy-done.1
  (15 shorter events, 0.1 us)
Async XLA Ops:
  7.2 9.6 %copy-start = (s32[12288]{0:T(1024)S(1)}, s32[12288]{0:T(1024)}, u32[]{:S(2)}) copy-start(s32[12288]{0:T(1024)} %param.8) | copy-start | bytes 147460
  11.6 9.8 %all-to-all-start = ((s32[8,22,1]{1,2,0:T(1,128)}), s32[8,22,1]{1,2,0:T(1,128)S(1)}, u32[]{:S(2)}, u32[]{:S(2)}) async-start(s32[8,22,1]{1,2,0:T(1,128)} %bitcast.2), calls=%async_computation | async-start | bytes 8192 | tf_op jit(solution)/shard_map/all_to_all | solution.py:71
  21.4 14.8 %all-to-all-start.1 = ((s32[8,22,128]{2,1,0:T(8,128)}), s32[8,22,128]{2,1,0:T(8,128)S(1)}, u32[]{:S(2)}, u32[]{:S(2)}) async-start(s32[8,22,128]{2,1,0:T(8,128)} %all_to_all.31), calls=%async_computation.1 | async-start | bytes 196608 | tf_op jit(solution)/shard_map/all_to_all | solution.py:72
  36.1 65.5 %all-to-all-start.2 = ((bf16[176,8,128]{2,1,0:T(8,128)(2,1)}), bf16[176,8,128]{2,1,0:T(8,128)(2,1)S(1)}, u32[]{:S(2)}, u32[]{:S(2)}) async-start(bf16[176,8,128]{2,1,0:T(8,128)(2,1)} %scatter_fusion), calls=%async_computation.2 | async-start | bytes 720896 | tf_op jit(solution)/shard_map/all_to_all | solution.py:73
  101.6 6.5 %copy-start.2 = (s32[80]{0:T(128)S(1)}, s32[80]{0:T(128)}, u32[]{:S(2)}) copy-start(s32[80]{0:T(128)} %param.12) | copy-start | bytes 964
  101.6 6.7 %copy-start.3 = (s32[8]{0:T(128)S(1)}, s32[8]{0:T(128)}, u32[]{:S(2)}) copy-start(s32[8]{0:T(128)} %param.10) | copy-start | bytes 100
  101.6 257.8 %all-to-all-start.3 = ((bf16[176,128,512]{2,1,0:T(8,128)(2,1)}), bf16[176,128,512]{2,1,0:T(8,128)(2,1)}, u32[]{:S(2)}, u32[]{:S(2)}) async-start(bf16[176,128,512]{2,1,0:T(8,128)(2,1)} %scatter_fusion.1), calls=%async_computation.3 | async-start | bytes 46137344 | tf_op jit(solution)/shard_map/all_to_all | solution.py:70
  448.9 58.7 %all-to-all-start.4 = ((bf16[19,128,2,256]{3,2,0,1:T(2,128)(2,1)}), bf16[19,128,2,256]{3,2,0,1:T(2,128)(2,1)S(1)}, u32[]{:S(2)}, u32[]{:S(2)}) async-start(bf16[19,128,2,256]{3,2,0,1:T(2,128)(2,1)} %copy.19), calls=%async_computation.4 | async-start | bytes 4980736 | tf_op jit(solution)/shard_map/all_to_all | solution.py:82
  453.8 107.4 %all-reduce.2.cloned.1.call-start = ((), (), s32[]{:S(2)}) async-start(), calls=%async_computation.5 | async-start | bytes 196608 | tf_op jit(solution)/shard_map/psum | solution.py:91
  510.2 14.1 %slice-start = ((s8[4980736]{0:T(1024)(128)(4,1)}), s8[786432]{0:T(1024)(128)(4,1)S(1)}, s32[]{:S(2)}) async-start(s8[4980736]{0:T(1024)(128)(4,1)} %bitcast.41), calls=%async_computation.6 | async-start | bytes 1572864
  513.3 11.1 %slice-start.1 = ((s8[4980736]{0:T(1024)(128)(4,1)}), s8[4194304]{0:T(1024)(128)(4,1)S(1)}, s32[]{:S(2)}) async-start(s8[4980736]{0:T(1024)(128)(4,1)} %bitcast.41), calls=%async_computation.7 | async-start | bytes 8388608
  513.3 49.4 %copy-start.1 = (s32[12288]{0:T(1024)S(1)}, s32[12288]{0:T(1024)}, u32[]{:S(2)}) copy-start(s32[12288]{0:T(1024)} %param.8) | copy-start | bytes 147460
Sparse Core Ops, SparseCore 0:
  526.5 34.6 all-reduce.1
where the time goes:
time: 572 us; the launch traced here: 570 us
  waiting for transfers between devices  311 us (54%)
  local copies, waits for them, and re-layouts  96.4 us (17%)
  matrix products  89.8 us (16%)
  other arithmetic  34.3 us (6%)
  starting transfers between devices  24 us (4%)
  between operations  14.3 us (2%)
    all_to_all x1, waiting for transfers between devices, body(): lax.all_to_all(sent_vis, 'uv', split_axis=0, concat_axis=0, tiled=True)  243 us
    dot_general x1, matrix products, body(): jnp.einsum('bs,bcf->scf', pick, contrib, precision=lax.Precision.HIGHEST)  49.7 us
    psum x1, waiting for transfers between devices, body(): power = lax.psum(local_power, 'chan') / jnp.float32(math.sqrt(TC))  34.8 us
    scatter x1, local copies, waits for them, and re-layouts, body(): jnp.zeros((buffer_size, BR, 2 * chan_dev), jnp.bfloat16).at[place]  33 us
    all_to_all x1, waiting for transfers between devices, body(): lax.all_to_all(gridded, 'chan', split_axis=1, concat_axis=3, tiled=True)  30.1 us
    dot_general x1, matrix products, body(): jnp.einsum('bcr,brf->bcf', got_matrix, got_vis, preferred_element_type=jn...  29 us
    reshape x1, local copies, waits for them, and re-layouts, body(): blocks = vis.reshape(nblocks, BR, 2 * chan_dev)  20.5 us
    another operation x1, other arithmetic  19.1 us
  transfers between devices with their start and end apart: 6, of which 4 were waited for; matrix products, arithmetic and copies ran while one was open for 19% of the time, Pallas kernels for 0%

commit v1 on v0

--- a/solution.py
+++ b/solution.py
@@ -88,7 +88,7 @@
     galaxy_f = galaxy.astype(jnp.float32)
     product = delay[..., :CH] * galaxy_f[..., :CH] + delay[..., CH:] * galaxy_f[..., CH:]
     local_power = jnp.sum(product, axis=1)
-    power = lax.psum(local_power, "chan") / jnp.float32(math.sqrt(TC))
+    power = jnp.sum(lax.all_gather(local_power, "chan"), axis=0) / jnp.float32(math.sqrt(TC))
     return (delay.astype(jnp.bfloat16), power)
 
 

time: 572 us -> 538 us (0.941)
  waiting for transfers between devices: 311 us -> 276 us
  blocking collectives: 0 us -> 14.8 us
  between operations: 14.3 us -> 0.88 us
    psum x1 -> x0, waiting for transfers between devices: 34.8 us -> none  [body(): power = lax.psum(local_power, 'chan') / jnp.float32(math.sqrt(TC))]
    all_gather x0 -> x1, blocking collectives: none -> 14.8 us  [body(): lax.all_gather(local_power, 'chan')]
  transfers between devices with their start and end apart: 6 -> 5, of which waited for: 4 -> 3; matrix products, arithmetic and copies ran while one was open for 19% -> 20% of each run, Pallas kernels for 0% -> 0%
where the time goes in v1:
time: 538 us; the launch traced here: 535 us
  waiting for transfers between devices  276 us (51%)
  local copies, waits for them, and re-layouts  96.4 us (18%)
  matrix products  89.8 us (17%)
  other arithmetic  32.8 us (6%)
  starting transfers between devices  24 us (4%)
  blocking collectives  14.8 us (3%)
    all_to_all x1, waiting for transfers between devices, body(): lax.all_to_all(sent_vis, 'uv', split_axis=0, concat_axis=0, tiled=True)  243 us
    dot_general x1, matrix products, body(): jnp.einsum('bs,bcf->scf', pick, contrib, precision=lax.Precision.HIGHEST)  49.7 us
    scatter x1, local copies, waits for them, and re-layouts, body(): jnp.zeros((buffer_size, BR, 2 * chan_dev), jnp.bfloat16).at[place]  33 us
    all_to_all x1, waiting for transfers between devices, body(): lax.all_to_all(gridded, 'chan', split_axis=1, concat_axis=3, tiled=True)  30.1 us
    dot_general x1, matrix products, body(): jnp.einsum('bcr,brf->bcf', got_matrix, got_vis, preferred_element_type=jn...  29 us
    reshape x1, local copies, waits for them, and re-layouts, body(): blocks = vis.reshape(nblocks, BR, 2 * chan_dev)  20.5 us
    another operation x1, other arithmetic  19.1 us
    all_gather x1, blocking collectives, body(): lax.all_gather(local_power, 'chan')  14.8 us
  transfers between devices with their start and end apart: 5, of which 3 were waited for; matrix products, arithmetic and copies ran while one was open for 20% of the time, Pallas kernels for 0%

profile of v1, /device:TPU:0, one launch (start us, length us, event | category | flops | bytes accessed | tf_op | source)
XLA Modules:
  0.0 534.6 jit_solution(15335371081919470968)
XLA Ops:
  0.6 0.0 copy-start
  0.6 0.7 compare_select_fusion.1
  1.3 1.6 gather_fusion
  2.9 0.1 fusion.41
  3.0 0.1 reduce_window_sum.22
  3.1 0.2 select_reduce_fusion
  3.3 1.0 scatter_custom_fusion
  4.3 0.7 all_to_all.29
  5.0 5.2 all-to-all-start
  10.2 0.0 copy-done
  10.2 0.8 scatter_custom_fusion.1
  11.1 0.6 all_to_all.31
  11.7 3.1 all-to-all-done
  14.8 3.4 all-to-all-start.1
  18.2 0.8 broadcast_in_dim.144
  19.0 10.6 %scatter_fusion = bf16[176,8,128]{2,1,0:T(8,128)(2,1)} fusion(bf16[176,8,128]{2,1,0:T(8,128)(2,1)} %broadcast_in_dim.144, s32[96]{0:T(128)S(1)} %fusion.47, bf16[96,8,128]{2,1,0:T(8,128)(2,1)} %bitcast.47), kind=kCustom, calls=%fused_computation.4 | custom fusion | bytes 590208 | tf_op jit(solution)/shard_map/scatter | solution.py:68
  29.6 0.0 all-to-all-done.1
  29.6 4.1 all-to-all-start.2
  33.7 20.5 %reshape.204 = bf16[96,128,512]{2,1,0:T(8,128)(2,1)} reshape(bf16[12288,2,256]{2,1,0:T(2,128)(2,1)} %param.7) | data formatting | bytes 25165824 | tf_op jit(solution)/shard_map/reshape | solution.py:62
  54.2 7.9 %broadcast_in_dim.170 = bf16[176,128,512]{2,1,0:T(8,128)(2,1)} broadcast(bf16[]{:T(256)} %constant.24.clone.1), dimensions={} | broadcast | bytes 23068674 | tf_op jit(solution)/shard_map/broadcast_in_dim | solution.py:65
  62.1 33.0 %scatter_fusion.1 = bf16[176,128,512]{2,1,0:T(8,128)(2,1)} fusion(bf16[176,128,512]{2,1,0:T(8,128)(2,1)} %broadcast_in_dim.170, s32[96]{0:T(128)S(1)} %fusion.47, bf16[96,128,512]{2,1,0:T(8,128)(2,1)} %reshape.204), kind=kCustom, calls=%fused_computation.5 | custom fusion | bytes 37749120 | tf_op jit(solution)/shard_map/scatter | solution.py:65
  95.1 0.0 copy-start.2
  95.1 0.0 copy-start.3
  95.1 0.0 all-to-all-done.2
  95.1 6.4 %all-to-all-start.3 = ((bf16[176,128,512]{2,1,0:T(8,128)(2,1)}), bf16[176,128,512]{2,1,0:T(8,128)(2,1)}, u32[]{:S(2)}, u32[]{:S(2)}) async-start(bf16[176,128,512]{2,1,0:T(8,128)(2,1)} %scatter_fusion.1), calls=%async_computation.3 | async-start | bytes 46137344 | tf_op jit(solution)/shard_map/all_to_all | solution.py:70
  101.5 0.0 copy-done.2
  101.5 0.1 fusion.43
  101.6 0.1 reduce_window_sum.23
  101.7 0.0 copy-done.3
  101.7 0.7 fusion.52
  102.4 0.2 select_reduce_fusion.1
  102.6 0.1 reshape.170
  102.7 0.1 ge.11
  102.8 1.6 gather_fusion.1
  104.4 5.1 broadcast_add_fusion.7
  109.6 0.5 slice_convert_fusion.7
  110.1 242.7 %all-to-all-done.3 = bf16[176,128,512]{2,1,0:T(8,128)(2,1)} async-done(((bf16[176,128,512]{2,1,0:T(8,128)(2,1)}), bf16[176,128,512]{2,1,0:T(8,128)(2,1)}, u32[]{:S(2)}, u32[]{:S(2)}) %all-to-all-start.3) | async-done | bytes 23068704 | tf_op jit(solution)/shard_map/all_to_all | solution.py:70
  352.8 29.0 %fusion.9 = f32[176,128,512]{2,1,0:T(8,128)} fusion(bf16[176,128,512]{2,1,0:T(8,128)(2,1)} %all-to-all-done.3, f32[176,128]{1,0:T(8,128)S(1)} %bitcast.49, s32[176,128]{1,0:T(8,128)S(1)} %add.221, f32[176,128]{1,0:T(8,128)S(1)} %bitcast.50, s32[176,128]{1,0:T(8,128)S(1)} %add.217, f32[176,128]{1,0:T(8,128)S(1)} %bitcast.51, s32[176,128]{1,0:T(8,128)S(1)} %add.213, ...), kind=kOutput, calls=%fused_computation.28 | convolution fusion | flops 3021996032 | bytes 70647808 | tf_op jit(solution)/shard_map/bcr,brf->bcf/dot_general | solution.py:76
  381.8 49.7 %fusion.35 = bf16[19,128,512]{2,0,1:T(8,128)(2,1)S(1)} fusion(f32[176,128,512]{2,1,0:T(8,128)} %fusion.9, s32[176]{0:T(256)S(1)} %broadcast_select_fusion), kind=kOutput, calls=%fused_computation.59 | convolution fusion | flops 2631077120 | bytes 48628416 | tf_op jit(solution)/shard_map/bs,bcf->scf/dot_general | solution.py:79
  431.5 3.4 copy.18
  435.0 7.4 %copy.19 = bf16[19,128,2,256]{3,2,0,1:T(2,128)(2,1)} copy(bf16[19,128,2,256]{1,3,2,0:T(8,128)(2,1)} %bitcast.44) | data formatting | bytes 4980736 | tf_op jit(solution)/shard_map/reshape | solution.py:80
  442.4 4.9 all-to-all-start.4
  447.3 4.6 convert_element_type.65
  451.8 0.1 subtract_multiply_fusion
  451.9 19.1 %multiply_convert_fusion.1 = (bf16[1024,1024]{1,0:T(8,128)(2,1)}, bf16[1024,1024]{1,0:T(8,128)(2,1)}, bf16[1024,1024]{1,0:T(8,128)(2,1)}) fusion(f32[1024]{0:T(1024)S(1)} %subtract_multiply_fusion), kind=kLoop, calls=%fused_computation.50 | loop fusion | flops 22020096 | bytes 6295552 | tf_op jit(solution)/shard_map/convert.13
  471.0 30.1 %all-to-all-done.4 = bf16[19,128,2,256]{3,2,0,1:T(2,128)(2,1)S(1)} async-done(((bf16[19,128,2,256]{3,2,0,1:T(2,128)(2,1)}), bf16[19,128,2,256]{3,2,0,1:T(2,128)(2,1)S(1)}, u32[]{:S(2)}, u32[]{:S(2)}) %all-to-all-start.4) | async-done | bytes 2490400 | tf_op jit(solution)/shard_map/all_to_all | solution.py:82
  501.1 0.4 copy.20
  501.5 2.2 copy.21
  503.7 0.0 slice-start
  503.7 3.0 dot_general.13
  506.7 0.0 slice-start.1
  506.7 0.0 copy-start.1
  506.7 11.1 %fusion.53 = (bf16[19,32,2048]{2,1,0:T(8,128)(2,1)}, f32[19,32,2048]{2,1,0:T(8,128)S(1)}) fusion(bf16[19,32,2048]{2,1,0:T(8,128)(2,1)} %dot_general.13, bf16[1024,1024]{1,0:T(8,128)(2,1)} %get-tuple-element.20, bf16[1024,1024]{1,0:T(8,128)(2,1)} %get-tuple-element.19, bf16[1024,1024]{1,0:T(8,128)(2,1)} %get-tuple-element.18), kind=kOutput, calls=%fused_computation.104 | convolution fusion | flops 5135073280 | bytes 16252928 | tf_op jit(solution)/shard_map/dot_general | solution.py:86
  517.8 0.0 slice-done
  517.8 0.0 slice-done.1
  517.8 1.4 fusion.34
  519.2 14.8 %all-gather.1 = f32[4,19,1024]{2,1,0:T(8,128)S(1)} all-gather(f32[1,19,1024]{2,1,0:T(8,128)S(1)} %bitcast.46), channel_id=2, replica_groups=mesh['uv'=8,'chan'=4] {'chan'}, dimensions={0}, use_global_device_ids=true | all-gather | bytes 389120 | tf_op jit(solution)/shard_map/all_gather | solution.py:91
  533.9 0.7 broadcast_multiply_fusion
  534.6 0.0 copy-done.1
  (16 shorter events, 0.2 us)
Async XLA Ops:
  0.6 9.6 %copy-start = (s32[12288]{0:T(1024)S(1)}, s32[12288]{0:T(1024)}, u32[]{:S(2)}) copy-start(s32[12288]{0:T(1024)} %param.8) | copy-start | bytes 147460
  5.0 9.8 %all-to-all-start = ((s32[8,22,1]{1,2,0:T(1,128)}), s32[8,22,1]{1,2,0:T(1,128)S(1)}, u32[]{:S(2)}, u32[]{:S(2)}) async-start(s32[8,22,1]{1,2,0:T(1,128)} %bitcast.2), calls=%async_computation | async-start | bytes 8192 | tf_op jit(solution)/shard_map/all_to_all | solution.py:71
  14.8 14.8 %all-to-all-start.1 = ((s32[8,22,128]{2,1,0:T(8,128)}), s32[8,22,128]{2,1,0:T(8,128)S(1)}, u32[]{:S(2)}, u32[]{:S(2)}) async-start(s32[8,22,128]{2,1,0:T(8,128)} %all_to_all.31), calls=%async_computation.1 | async-start | bytes 196608 | tf_op jit(solution)/shard_map/all_to_all | solution.py:72
  29.6 65.5 %all-to-all-start.2 = ((bf16[176,8,128]{2,1,0:T(8,128)(2,1)}), bf16[176,8,128]{2,1,0:T(8,128)(2,1)S(1)}, u32[]{:S(2)}, u32[]{:S(2)}) async-start(bf16[176,8,128]{2,1,0:T(8,128)(2,1)} %scatter_fusion), calls=%async_computation.2 | async-start | bytes 720896 | tf_op jit(solution)/shard_map/all_to_all | solution.py:73
  95.1 6.5 %copy-start.2 = (s32[80]{0:T(128)S(1)}, s32[80]{0:T(128)}, u32[]{:S(2)}) copy-start(s32[80]{0:T(128)} %param.12) | copy-start | bytes 964
  95.1 6.7 %copy-start.3 = (s32[8]{0:T(128)S(1)}, s32[8]{0:T(128)}, u32[]{:S(2)}) copy-start(s32[8]{0:T(128)} %param.10) | copy-start | bytes 100
  95.1 257.8 %all-to-all-start.3 = ((bf16[176,128,512]{2,1,0:T(8,128)(2,1)}), bf16[176,128,512]{2,1,0:T(8,128)(2,1)}, u32[]{:S(2)}, u32[]{:S(2)}) async-start(bf16[176,128,512]{2,1,0:T(8,128)(2,1)} %scatter_fusion.1), calls=%async_computation.3 | async-start | bytes 46137344 | tf_op jit(solution)/shard_map/all_to_all | solution.py:70
  442.4 58.7 %all-to-all-start.4 = ((bf16[19,128,2,256]{3,2,0,1:T(2,128)(2,1)}), bf16[19,128,2,256]{3,2,0,1:T(2,128)(2,1)S(1)}, u32[]{:S(2)}, u32[]{:S(2)}) async-start(bf16[19,128,2,256]{3,2,0,1:T(2,128)(2,1)} %copy.19), calls=%async_computation.4 | async-start | bytes 4980736 | tf_op jit(solution)/shard_map/all_to_all | solution.py:82
  503.7 14.1 %slice-start = ((s8[4980736]{0:T(1024)(128)(4,1)}), s8[786432]{0:T(1024)(128)(4,1)S(1)}, s32[]{:S(2)}) async-start(s8[4980736]{0:T(1024)(128)(4,1)} %bitcast.42), calls=%async_computation.5 | async-start | bytes 1572864
  506.7 11.1 %slice-start.1 = ((s8[4980736]{0:T(1024)(128)(4,1)}), s8[4194304]{0:T(1024)(128)(4,1)S(1)}, s32[]{:S(2)}) async-start(s8[4980736]{0:T(1024)(128)(4,1)} %bitcast.42), calls=%async_computation.6 | async-start | bytes 8388608
  506.7 27.9 %copy-start.1 = (s32[12288]{0:T(1024)S(1)}, s32[12288]{0:T(1024)}, u32[]{:S(2)}) copy-start(s32[12288]{0:T(1024)} %param.8) | copy-start | bytes 147460
